TPU v7x, 512 devices: a whole 4x8x8 slice. The times are simulated.
512 devices in a mesh: dp: 16 (over y, core), comp: 32 (over z, x).
Axes of the slice: x: 4, y: 8, z: 8, core: 2. Of those that a mesh axis runs over, the one named last changes fastest.
Arguments:
- descriptors: bfloat16 [65536, 256], P('dp'), may hold values from -12 to 12
- means: float32 [16384, 256], P('comp'), may hold values from -3 to 3
- variances: float32 [16384, 256], P('comp'), may hold values from 0.5 to 2
- log_weights: float32 [16384], P('comp'), may hold values from -2 to 2
Outputs:
- new_log_weights: float32 [16384], P('comp')
- new_means: float32 [16384, 256], P('comp')
- new_variances: float32 [16384, 256], P('comp')
All inputs are finite; a program needn't handle non-finite values.
Results may differ from a plain program's by a relative error of at most 0.002.
Values sent between devices are 32-bit elements; how exact they have to be, the bound alone decides.
No kernel may reach another device: no remote copies, remote signals or barrier semaphores. Data moves between devices by JAX's collectives and lax.ppermute only.
A program may use at most 64 MiB of HBM per device.

v0:
```python
import jax
import jax.numpy as jnp
from jax import lax
from jax.sharding import PartitionSpec as P

prior_count = 1.0
log_two_pi = 1.8378770664093453


def finish(moments, counts, means, variances, grand_total):
    feature_width = means.shape[1]
    weight = counts + prior_count
    new_means = (moments[:, :feature_width] + prior_count * means) / weight[:, None]
    new_variances = (
        moments[:, feature_width:] + prior_count * (variances + means * means)
    ) / weight[:, None] - new_means * new_means
    new_log_weights = jnp.log(weight) - jnp.log(grand_total)
    return (new_log_weights, new_means, new_variances)


def on_device(descriptors, means, variances, log_weights):
    row_count = descriptors.shape[0]
    feature_width = descriptors.shape[1]
    owned_count = means.shape[0]
    grand_total = row_count * lax.axis_size("dp") + prior_count * owned_count * lax.axis_size(
        "comp"
    )
    precision = 1.0 / variances
    scaled_means = means * precision
    loading = jnp.concatenate([-0.5 * precision, scaled_means], axis=1)
    offset = log_weights - 0.5 * jnp.sum(
        means * scaled_means + jnp.log(variances) + log_two_pi, axis=1
    )
    block_rows = min(512, row_count)
    stacked = descriptors.reshape(row_count // block_rows, block_rows, feature_width)

    def score_block(row_block):
        exact = row_block.astype(jnp.float32)
        features = jnp.concatenate([exact * exact, exact], axis=1)
        return (
            lax.dot_general(
                features,
                loading,
                (((1,), (1,)), ((), ())),
                precision=lax.Precision.HIGHEST,
                preferred_element_type=jnp.float32,
            )
            + offset[None, :]
        )

    scores = lax.map(score_block, stacked).reshape(row_count, owned_count)
    row_max = lax.pmax(jnp.max(scores, axis=1), "comp")
    row_sum = lax.psum(jnp.sum(jnp.exp(scores - row_max[:, None]), axis=1), "comp")
    log_total = row_max + jnp.log(row_sum)
    responsibility = jnp.exp(scores - log_total[:, None])
    counts = jnp.sum(responsibility, axis=0)
    resp_half = responsibility.astype(jnp.bfloat16)
    exact_rows = descriptors.astype(jnp.float32)
    halves = jnp.concatenate([descriptors, (exact_rows * exact_rows).astype(jnp.bfloat16)], axis=1)
    moments = lax.dot_general(
        resp_half, halves, (((0,), (0,)), ((), ())), preferred_element_type=jnp.float32
    )
    summed_moments, summed_counts = lax.psum((moments, counts), "dp")
    new_log_weights, new_means, new_variances = finish(
        summed_moments, summed_counts, means, variances, grand_total
    )
    return (new_log_weights, new_means, new_variances)


def solution(mesh):
    placed = (P("dp", None), P("comp", None), P("comp", None), P("comp"))
    return jax.shard_map(
        on_device,
        mesh=mesh,
        in_specs=placed,
        out_specs=(P("comp"), P("comp", None), P("comp", None)),
        check_vma=False,
    )
```

profile of v0, /device:TPU:1, one launch (start us, length us, event | category | flops | bytes accessed | tf_op | source)
XLA Modules:
  0.0 460.0 jit_solution(11352308650413129347)
XLA Ops:
  7.2 0.0 copy-start
  7.2 0.0 copy-start.4
  7.2 0.0 all-reduce.2.cloned.1.call-start
  7.2 3.5 multiply_convert_fusion
  10.8 1.5 add_reduce_fusion
  12.2 0.1 pad_maximum_fusion
  12.4 0.0 copy-done.4
  12.4 0.0 copy-done
  12.4 23.7 %while.10 = (s32[]{:T(128)}, f32[8,512,512]{2,1,0:T(8,128)}, bf16[8,512,256]{2,1,0:T(8,128)(2,1)S(1)}, f32[512,512]{1,0:T(8,128)S(1)}, f32[512]{0:T(512)S(1)}, /*index=5*/s32[]{:T(128)}) while((s32[]{:T(128)}, f32[8,512,512]{2,1,0:T(8,128)}, bf16[8,512,256]{2,1,0:T(8,128)(2,1)S(1)}, f32[512,512]{1,0:T(8,128)S(1)}, f32[512]{0:T(512)S(1)}, ...), condition=%wide.region_2.3_spmd, body=%wide.region_1.2_spmd.sunk | while | flops 1611530240 | bytes 4721229 | solution.py:51
  12.5 2.9 fusion.28
  15.5 2.9 fusion.28
  18.5 2.9 fusion.28
  21.4 2.9 fusion.28
  24.4 2.8 fusion.28
  27.3 2.9 fusion.28
  30.3 2.9 fusion.28
  33.3 2.8 fusion.28
  36.1 4.0 reduce_max.11
  40.2 121.8 %pmax.7 = f32[4096]{0:T(1024)S(1)} all-reduce(f32[4096]{0:T(1024)S(1)} %bitcast.34), channel_id=1, replica_groups=mesh['dp'=16,'comp'=32] {'comp'}, use_global_device_ids=true, to_apply=%region_4.5 | all-reduce | flops 4096 | bytes 32768 | tf_op jit(solution)/shard_map/pmax | solution.py:52
  162.0 4.4 exponential_reduce_fusion.1
  166.4 110.4 %psum.21 = f32[4096]{0:T(1024)S(1)} all-reduce(f32[4096]{0:T(1024)S(1)} %bitcast.35), channel_id=1, replica_groups=mesh['dp'=16,'comp'=32] {'comp'}, use_global_device_ids=true, to_apply=%region_6.7 | all-reduce | flops 4096 | bytes 32768 | tf_op jit(solution)/shard_map/psum | solution.py:53
  276.8 0.0 copy-start.1
  276.8 4.2 fusion.8
  281.1 0.0 copy-done.1
  281.1 3.3 fusion.9
  284.4 0.0 copy-start.2
  284.4 0.0 copy-start.3
  284.4 0.0 all-reduce.2.cloned.1.call-update
  284.5 4.2 exponential_reduce_fusion
  288.6 79.3 %psum.22 = f32[512]{0:T(512)S(1)} all-reduce(f32[512]{0:T(512)S(1)} %exponential_reduce_fusion), channel_id=1, replica_groups=mesh['dp'=16,'comp'=32] {'dp'}, use_global_device_ids=true, to_apply=%region_8.9 | all-reduce | flops 512 | bytes 4096 | tf_op jit(solution)/shard_map/psum | solution.py:63
  368.0 0.6 broadcast_add_fusion
  368.6 82.2 %all-reduce.2.cloned.1.call-done = f32[512,512]{1,0:T(8,128)} async-done(((f32[512,512]{1,0:T(8,128)}), f32[512,512]{1,0:T(8,128)}) %all-reduce.2.cloned.1.call-update) | async-done | bytes 1048592 | tf_op jit(solution)/shard_map/psum | solution.py:63
  450.8 0.0 copy-done.2
  450.8 0.0 copy-done.3
  450.8 2.4 fusion.14
  (23 shorter events, 0.7 us)
Async XLA Ops:
  7.2 5.3 %copy-start = (bf16[4096,256]{1,0:T(8,128)(2,1)S(1)}, bf16[4096,256]{1,0:T(8,128)(2,1)}, u32[]{:S(2)}) copy-start(bf16[4096,256]{1,0:T(8,128)(2,1)} %param.6) | copy-start | bytes 6291460
  7.2 5.2 %copy-start.4 = (f32[512]{0:T(512)S(1)}, f32[512]{0:T(512)}, u32[]{:S(2)}) copy-start(f32[512]{0:T(512)} %param.9) | copy-start | bytes 6148
  7.2 443.6 %all-reduce.2.cloned.1.call-start = ((), (), s32[]{:S(2)}) async-start(), calls=%async_computation | async-start | bytes 2097152 | tf_op jit(solution)/shard_map/psum | solution.py:63
  276.8 4.3 copy-start.1
  284.4 166.3 %copy-start.2 = (f32[512,256]{1,0:T(8,128)S(1)}, f32[512,256]{1,0:T(8,128)}, u32[]{:S(2)}) copy-start(f32[512,256]{1,0:T(8,128)} %param.8) | copy-start | bytes 1572868
  284.4 166.3 %copy-start.3 = (f32[512,256]{1,0:T(8,128)S(1)}, f32[512,256]{1,0:T(8,128)}, u32[]{:S(2)}) copy-start(f32[512,256]{1,0:T(8,128)} %param.7) | copy-start | bytes 1572868
Sparse Core Ops, SparseCore 0:
  284.6 166.1 all-reduce.1
where the time goes:
time: 460 us
  blocking collectives  312 us (68%)
  waiting for transfers between devices  82.2 us (18%)
  matrix products  26.3 us (6%)
  other arithmetic  25.6 us (6%)
  between operations  14.1 us (3%)
    pmax x1, blocking collectives, on_device(): row_max = lax.pmax(jnp.max(scores, axis=1), 'comp')  122 us
    psum x1, blocking collectives, on_device(): lax.psum(jnp.sum(jnp.exp(scores - row_max[:, None]), axis=1), 'comp')  110 us
    psum x1, waiting for transfers between devices, on_device(): summed_moments, summed_counts = lax.psum((moments, counts), 'dp')  82.2 us
    psum x1, blocking collectives, on_device(): summed_moments, summed_counts = lax.psum((moments, counts), 'dp')  79.3 us
    dot_general x8, matrix products, score_block(): lax.dot_general(features, loading, (((1,), (1,)), ((), ())), precision=la...  22.9 us
  transfers between devices with their start and end apart: 1, of which 1 were waited for; matrix products, arithmetic and copies ran while one was open for 1% of the time, Pallas kernels for 0%

commit v1 on v0

--- a/solution.py
+++ b/solution.py
@@ -49,8 +49,11 @@
         )
 
     scores = lax.map(score_block, stacked).reshape(row_count, owned_count)
-    row_max = lax.pmax(jnp.max(scores, axis=1), "comp")
-    row_sum = lax.psum(jnp.sum(jnp.exp(scores - row_max[:, None]), axis=1), "comp")
+    local_max = jnp.max(scores, axis=1)
+    local_sum = jnp.sum(jnp.exp(scores - local_max[:, None]), axis=1)
+    gathered = lax.all_gather(jnp.stack([local_max, local_sum]), "comp")
+    row_max = jnp.max(gathered[:, 0], axis=0)
+    row_sum = jnp.sum(gathered[:, 1] * jnp.exp(gathered[:, 0] - row_max[None, :]), axis=0)
     log_total = row_max + jnp.log(row_sum)
     responsibility = jnp.exp(scores - log_total[:, None])
     counts = jnp.sum(responsibility, axis=0)
@@ -60,7 +63,9 @@
     moments = lax.dot_general(
         resp_half, halves, (((0,), (0,)), ((), ())), preferred_element_type=jnp.float32
     )
-    summed_moments, summed_counts = lax.psum((moments, counts), "dp")
+    packed = lax.psum(jnp.concatenate([moments, counts[None, :]], axis=0), "dp")
+    summed_moments = packed[:owned_count]
+    summed_counts = packed[owned_count]
     new_log_weights, new_means, new_variances = finish(
         summed_moments, summed_counts, means, variances, grand_total
     )

time: 460 us -> 273 us (0.59)
  blocking collectives: 312 us -> 0 us
  waiting for transfers between devices: 82.2 us -> 200 us
  other arithmetic: 25.6 us -> 31.3 us
    psum x2 -> x0, blocking collectives: 190 us -> none  [the longest x1 110 us: on_device(): lax.psum(jnp.sum(jnp.exp(scores - row_max[:, None]), axis=1), 'comp')]
    pmax x1 -> x0, blocking collectives: 122 us -> none  [on_device(): row_max = lax.pmax(jnp.max(scores, axis=1), 'comp')]
    all_gather x0 -> x1, waiting for transfers between devices: none -> 81 us  [on_device(): gathered = lax.all_gather(jnp.stack([local_max, local_sum]), 'comp')]
    psum x1, waiting for transfers between devices: 82.2 us -> 119 us  [on_device(): packed = lax.psum(jnp.concatenate([moments, counts[None, :]], axis=0), 'dp')]
  transfers between devices with their start and end apart: 1 -> 2, of which waited for: 1 -> 2; matrix products, arithmetic and copies ran while one was open for 1% -> 1% of each run, Pallas kernels for 0% -> 0%
where the time goes in v1:
time: 273 us; the launch traced here: 272 us
  waiting for transfers between devices  200 us (73%)
  other arithmetic  31.3 us (11%)
  matrix products  25.3 us (9%)
  between operations  14.2 us (5%)
    psum x1, waiting for transfers between devices, on_device(): packed = lax.psum(jnp.concatenate([moments, counts[None, :]], axis=0), 'dp')  119 us
    all_gather x1, waiting for transfers between devices, on_device(): gathered = lax.all_gather(jnp.stack([local_max, local_sum]), 'comp')  81 us
    dot_general x8, matrix products, score_block(): lax.dot_general(features, loading, (((1,), (1,)), ((), ())), precision=la...  22.9 us
  transfers between devices with their start and end apart: 2, of which 2 were waited for; matrix products, arithmetic and copies ran while one was open for 1% of the time, Pallas kernels for 0%

profile of v1, /device:TPU:1, one launch (start us, length us, event | category | flops | bytes accessed | tf_op | source)
XLA Modules:
  0.0 272.1 jit_solution(8249931385995249936)
XLA Ops:
  7.2 0.0 copy-start.5
  7.2 0.0 copy-start
  7.2 0.0 all-gather.4.cloned.1.call-start
  7.2 1.6 add_reduce_fusion
  8.8 0.1 pad_maximum_fusion.1
  9.0 0.0 copy-done.5
  9.0 0.1 copy-done
  9.1 23.7 %while.10 = (s32[]{:T(128)}, f32[8,512,512]{2,1,0:T(8,128)}, bf16[8,512,256]{2,1,0:T(8,128)(2,1)S(1)}, f32[512,512]{1,0:T(8,128)S(1)}, f32[512]{0:T(512)S(1)}, /*index=5*/s32[]{:T(128)}) while((s32[]{:T(128)}, f32[8,512,512]{2,1,0:T(8,128)}, bf16[8,512,256]{2,1,0:T(8,128)(2,1)S(1)}, f32[512,512]{1,0:T(8,128)S(1)}, f32[512]{0:T(512)S(1)}, ...), condition=%wide.region_2.3_spmd, body=%wide.region_1.2_spmd.sunk | while | flops 1611530240 | bytes 4721229 | solution.py:51
  9.2 2.9 %fusion.32 = f32[8,512,512]{2,1,0:T(8,128)} fusion(f32[8,512,512]{2,1,0:T(8,128)} %get-tuple-element.87, s32[]{:T(128)} %get-tuple-element.86, f32[512,512]{1,0:T(8,128)S(1)} %get-tuple-element.95, f32[512,256]{1,0:T(8,128)S(1)} %bitcast_convert_fusion.2, f32[512,256]{1,0:T(8,128)S(1)} %fusion.31, f32[512]{0:T(512)S(1)} %get-tuple-element.96), kind=kOutput, calls=%fused_computation.2.clone.1 | convolution fusion | flops 1611137024 | bytes 3148288 | tf_op jit(solution)/shard_map/while/body/eval_jaxpr/dot_general | solution.py:41
  12.1 2.9 %fusion.32 = f32[8,512,512]{2,1,0:T(8,128)} fusion(f32[8,512,512]{2,1,0:T(8,128)} %get-tuple-element.87, s32[]{:T(128)} %get-tuple-element.86, f32[512,512]{1,0:T(8,128)S(1)} %get-tuple-element.95, f32[512,256]{1,0:T(8,128)S(1)} %bitcast_convert_fusion.2, f32[512,256]{1,0:T(8,128)S(1)} %fusion.31, f32[512]{0:T(512)S(1)} %get-tuple-element.96), kind=kOutput, calls=%fused_computation.2.clone.1 | convolution fusion | flops 1611137024 | bytes 3148288 | tf_op jit(solution)/shard_map/while/body/eval_jaxpr/dot_general | solution.py:41
  15.1 2.9 %fusion.32 = f32[8,512,512]{2,1,0:T(8,128)} fusion(f32[8,512,512]{2,1,0:T(8,128)} %get-tuple-element.87, s32[]{:T(128)} %get-tuple-element.86, f32[512,512]{1,0:T(8,128)S(1)} %get-tuple-element.95, f32[512,256]{1,0:T(8,128)S(1)} %bitcast_convert_fusion.2, f32[512,256]{1,0:T(8,128)S(1)} %fusion.31, f32[512]{0:T(512)S(1)} %get-tuple-element.96), kind=kOutput, calls=%fused_computation.2.clone.1 | convolution fusion | flops 1611137024 | bytes 3148288 | tf_op jit(solution)/shard_map/while/body/eval_jaxpr/dot_general | solution.py:41
  18.1 2.9 %fusion.32 = f32[8,512,512]{2,1,0:T(8,128)} fusion(f32[8,512,512]{2,1,0:T(8,128)} %get-tuple-element.87, s32[]{:T(128)} %get-tuple-element.86, f32[512,512]{1,0:T(8,128)S(1)} %get-tuple-element.95, f32[512,256]{1,0:T(8,128)S(1)} %bitcast_convert_fusion.2, f32[512,256]{1,0:T(8,128)S(1)} %fusion.31, f32[512]{0:T(512)S(1)} %get-tuple-element.96), kind=kOutput, calls=%fused_computation.2.clone.1 | convolution fusion | flops 1611137024 | bytes 3148288 | tf_op jit(solution)/shard_map/while/body/eval_jaxpr/dot_general | solution.py:41
  21.0 2.8 %fusion.32 = f32[8,512,512]{2,1,0:T(8,128)} fusion(f32[8,512,512]{2,1,0:T(8,128)} %get-tuple-element.87, s32[]{:T(128)} %get-tuple-element.86, f32[512,512]{1,0:T(8,128)S(1)} %get-tuple-element.95, f32[512,256]{1,0:T(8,128)S(1)} %bitcast_convert_fusion.2, f32[512,256]{1,0:T(8,128)S(1)} %fusion.31, f32[512]{0:T(512)S(1)} %get-tuple-element.96), kind=kOutput, calls=%fused_computation.2.clone.1 | convolution fusion | flops 1611137024 | bytes 3148288 | tf_op jit(solution)/shard_map/while/body/eval_jaxpr/dot_general | solution.py:41
  24.0 2.9 %fusion.32 = f32[8,512,512]{2,1,0:T(8,128)} fusion(f32[8,512,512]{2,1,0:T(8,128)} %get-tuple-element.87, s32[]{:T(128)} %get-tuple-element.86, f32[512,512]{1,0:T(8,128)S(1)} %get-tuple-element.95, f32[512,256]{1,0:T(8,128)S(1)} %bitcast_convert_fusion.2, f32[512,256]{1,0:T(8,128)S(1)} %fusion.31, f32[512]{0:T(512)S(1)} %get-tuple-element.96), kind=kOutput, calls=%fused_computation.2.clone.1 | convolution fusion | flops 1611137024 | bytes 3148288 | tf_op jit(solution)/shard_map/while/body/eval_jaxpr/dot_general | solution.py:41
  27.0 2.9 %fusion.32 = f32[8,512,512]{2,1,0:T(8,128)} fusion(f32[8,512,512]{2,1,0:T(8,128)} %get-tuple-element.87, s32[]{:T(128)} %get-tuple-element.86, f32[512,512]{1,0:T(8,128)S(1)} %get-tuple-element.95, f32[512,256]{1,0:T(8,128)S(1)} %bitcast_convert_fusion.2, f32[512,256]{1,0:T(8,128)S(1)} %fusion.31, f32[512]{0:T(512)S(1)} %get-tuple-element.96), kind=kOutput, calls=%fused_computation.2.clone.1 | convolution fusion | flops 1611137024 | bytes 3148288 | tf_op jit(solution)/shard_map/while/body/eval_jaxpr/dot_general | solution.py:41
  29.9 2.8 %fusion.32 = f32[8,512,512]{2,1,0:T(8,128)} fusion(f32[8,512,512]{2,1,0:T(8,128)} %get-tuple-element.87, s32[]{:T(128)} %get-tuple-element.86, f32[512,512]{1,0:T(8,128)S(1)} %get-tuple-element.95, f32[512,256]{1,0:T(8,128)S(1)} %bitcast_convert_fusion.2, f32[512,256]{1,0:T(8,128)S(1)} %fusion.31, f32[512]{0:T(512)S(1)} %get-tuple-element.96), kind=kOutput, calls=%fused_computation.2.clone.1 | convolution fusion | flops 1611137024 | bytes 3148288 | tf_op jit(solution)/shard_map/while/body/eval_jaxpr/dot_general | solution.py:41
  32.8 4.0 %reduce_max.18 = f32[8,512]{1,0:T(8,128)S(1)} reduce(f32[8,512,512]{2,1,0:T(8,128)} %get-tuple-element.30, f32[]{:T(128)} %constant.10.clone.1), dimensions={2}, to_apply=%region_3.4 | reduce | flops 2093056 | bytes 8404996 | tf_op jit(solution)/shard_map/reduce_max | solution.py:52
  36.8 4.4 %exponential_reduce_fusion.1 = f32[8,512]{1,0:T(8,128)S(1)} fusion(f32[8,512,512]{2,1,0:T(8,128)} %get-tuple-element.30, f32[8,512]{1,0:T(8,128)S(1)} %reduce_max.18), kind=kLoop, calls=%fused_computation.13 | loop fusion | flops 4190208 | bytes 8421376 | tf_op jit(solution)/shard_map/reduce_sum | solution.py:53
  41.3 0.6 maximum_bitcast_fusion
  41.9 0.0 all-gather.4.cloned.1.call-update
  41.9 0.0 all-reduce.2.cloned.1.call-start
  42.0 1.8 multiply_convert_fusion
  43.8 81.0 %all-gather.4.cloned.1.call-done = f32[32,2,4096]{2,1,0:T(2,128)} async-done(((f32[1,2,4096]{2,1,0:T(2,128)}), f32[32,2,4096]{2,1,0:T(2,128)}) %all-gather.4.cloned.1.call-update) | async-done | bytes 1048592 | tf_op jit(solution)/shard_map/all_gather | solution.py:54
  124.8 2.9 %fusion.22 = (f32[32,1,4096]{2,1,0:T(1,128)S(1)}, f32[4096]{0:T(1024)S(1)}, f32[32,1,4096]{2,1,0:T(1,128)S(1)}) fusion(f32[32,2,4096]{2,1,0:T(2,128)} %all-gather.4.cloned.1.call-done), kind=kLoop, calls=%fused_computation.42 | loop fusion | flops 126976 | bytes 2113536 | tf_op jit(solution)/shard_map/slice | solution.py:55
  127.7 0.7 fusion.17
  128.4 5.4 %fusion.8 = bf16[4096,512]{1,0:T(8,128)(2,1)} fusion(f32[8,512,512]{2,1,0:T(8,128)} %get-tuple-element.30, f32[4096]{0:T(1024)S(1)} %log_add_fusion), kind=kLoop, calls=%fused_computation.11 | loop fusion | flops 4194304 | bytes 12599296 | tf_op jit(solution)/shard_map/convert_element_type | solution.py:60
  133.8 0.0 copy-start.1
  133.8 0.0 copy-start.2
  133.8 4.2 %exponential_reduce_fusion = f32[512]{0:T(512)S(1)} fusion(f32[8,512,512]{2,1,0:T(8,128)} %get-tuple-element.30, f32[8,512]{1,0:T(8,128)S(1)} %add.60), kind=kLoop, calls=%fused_computation.12 | loop fusion | flops 4193792 | bytes 8407040 | tf_op jit(solution)/shard_map/reduce_sum | solution.py:59
  138.1 0.4 copy-done.1
  138.5 0.7 copy-done.2
  139.2 0.0 copy-start.3
  139.2 0.0 copy-start.4
  139.2 2.3 fusion.9
  141.5 1.1 pad_maximum_fusion
  142.6 0.0 all-reduce.2.cloned.1.call-update
  142.7 119.0 %all-reduce.2.cloned.1.call-done = f32[513,512]{1,0:T(8,128)} async-done(((f32[513,512]{1,0:T(8,128)}), f32[513,512]{1,0:T(8,128)}) %all-reduce.2.cloned.1.call-update) | async-done | bytes 1050640 | tf_op jit(solution)/shard_map/psum | solution.py:66
  261.6 0.7 slice_add_fusion.2
  262.3 0.6 log_add_fusion.1
  262.9 0.0 copy-done.3
  262.9 0.0 copy-done.4
  262.9 2.4 fusion.14
  (22 shorter events, 0.7 us)
Async XLA Ops:
  7.2 1.8 copy-start.5
  7.2 1.9 copy-start
  7.2 117.6 %all-gather.4.cloned.1.call-start = ((), (), s32[]{:S(2)}) async-start(), calls=%async_computation.1 | async-start | bytes 1081344 | tf_op jit(solution)/shard_map/all_gather | solution.py:54
  41.9 219.7 %all-reduce.2.cloned.1.call-start = ((), (), s32[]{:S(2)}) async-start(), calls=%async_computation | async-start | bytes 2129920 | tf_op jit(solution)/shard_map/psum | solution.py:66
  133.8 4.6 %copy-start.1 = (bf16[4096,512]{1,0:T(8,128)(2,1)S(1)}, bf16[4096,512]{1,0:T(8,128)(2,1)}, u32[]{:S(2)}) copy-start(bf16[4096,512]{1,0:T(8,128)(2,1)} %fusion.8) | copy-start | bytes 12582916
  133.8 5.3 %copy-start.2 = (bf16[4096,256]{1,0:T(8,128)(2,1)S(1)}, bf16[4096,256]{1,0:T(8,128)(2,1)}, u32[]{:S(2)}) copy-start(bf16[4096,256]{1,0:T(8,128)(2,1)} %multiply_convert_fusion) | copy-start | bytes 6291460
  139.2 123.8 %copy-start.3 = (f32[512,256]{1,0:T(8,128)S(1)}, f32[512,256]{1,0:T(8,128)}, u32[]{:S(2)}) copy-start(f32[512,256]{1,0:T(8,128)} %param.8) | copy-start | bytes 1572868
  139.2 123.8 %copy-start.4 = (f32[512,256]{1,0:T(8,128)S(1)}, f32[512,256]{1,0:T(8,128)}, u32[]{:S(2)}) copy-start(f32[512,256]{1,0:T(8,128)} %param.7) | copy-start | bytes 1572868
Sparse Core Ops, SparseCore 0:
  42.1 82.6 all-gather.3
  142.8 118.7 all-reduce.1

commit v2 on v0

--- a/solution.py
+++ b/solution.py
@@ -16,6 +16,48 @@
     ) / weight[:, None] - new_means * new_means
     new_log_weights = jnp.log(weight) - jnp.log(grand_total)
     return (new_log_weights, new_means, new_variances)
+
+
+def xor_pairs(size, bit):
+    return [(i, i ^ bit) for i in range(size)]
+
+
+def row_logsumexp_stats(local_max, local_sum, axis):
+    size = lax.axis_size(axis)
+    row_max, row_sum = local_max, local_sum
+    bit = 1
+    while bit < size:
+        other = lax.ppermute(jnp.stack([row_max, row_sum]), axis, xor_pairs(size, bit))
+        other_max, other_sum = other[0], other[1]
+        new_max = jnp.maximum(row_max, other_max)
+        row_sum = row_sum * jnp.exp(row_max - new_max) + other_sum * jnp.exp(other_max - new_max)
+        row_max = new_max
+        bit *= 2
+    return row_max, row_sum
+
+
+def halving_psum(rows, axis):
+    size = lax.axis_size(axis)
+    index = lax.axis_index(axis)
+    current = rows
+    bits = []
+    bit = 1
+    while bit < size:
+        half = current.shape[0] // 2
+        low, high = current[:half], current[half:]
+        upper = (index // bit) % 2 == 1
+        keep = jnp.where(upper, high, low)
+        send = jnp.where(upper, low, high)
+        current = keep + lax.ppermute(send, axis, xor_pairs(size, bit))
+        bits.append(bit)
+        bit *= 2
+    for bit in reversed(bits):
+        upper = (index // bit) % 2 == 1
+        other = lax.ppermute(current, axis, xor_pairs(size, bit))
+        current = jnp.where(
+            upper, jnp.concatenate([other, current]), jnp.concatenate([current, other])
+        )
+    return current
 
 
 def on_device(descriptors, means, variances, log_weights):
@@ -49,8 +91,9 @@
         )
 
     scores = lax.map(score_block, stacked).reshape(row_count, owned_count)
-    row_max = lax.pmax(jnp.max(scores, axis=1), "comp")
-    row_sum = lax.psum(jnp.sum(jnp.exp(scores - row_max[:, None]), axis=1), "comp")
+    local_max = jnp.max(scores, axis=1)
+    local_sum = jnp.sum(jnp.exp(scores - local_max[:, None]), axis=1)
+    row_max, row_sum = row_logsumexp_stats(local_max, local_sum, "comp")
     log_total = row_max + jnp.log(row_sum)
     responsibility = jnp.exp(scores - log_total[:, None])
     counts = jnp.sum(responsibility, axis=0)
@@ -60,7 +103,22 @@
     moments = lax.dot_general(
         resp_half, halves, (((0,), (0,)), ((), ())), preferred_element_type=jnp.float32
     )
-    summed_moments, summed_counts = lax.psum((moments, counts), "dp")
+    lanes = 128
+    dp_size = lax.axis_size("dp")
+    flat_rows = (moments.size + counts.size) // lanes
+    unit = 8 * dp_size
+    padded_rows = -(-flat_rows // unit) * unit
+    packed = jnp.concatenate(
+        [
+            moments.reshape(-1, lanes),
+            counts.reshape(-1, lanes),
+            jnp.zeros((padded_rows - flat_rows, lanes), jnp.float32),
+        ]
+    )
+    summed = halving_psum(packed, "dp")
+    moment_rows = moments.size // lanes
+    summed_moments = summed[:moment_rows].reshape(moments.shape)
+    summed_counts = summed[moment_rows:flat_rows].reshape(counts.shape)
     new_log_weights, new_means, new_variances = finish(
         summed_moments, summed_counts, means, variances, grand_total
     )

time: 460 us -> 161 us (0.35)
  blocking collectives: 312 us -> 0 us
  starting transfers between devices: 0.04 us -> 58.7 us
  waiting for transfers between devices: 82.2 us -> 49.7 us
  between operations: 14.1 us -> 1.24 us
    psum x2 -> x0, blocking collectives: 190 us -> none  [the longest x1 110 us: on_device(): lax.psum(jnp.sum(jnp.exp(scores - row_max[:, None]), axis=1), 'comp')]
    pmax x1 -> x0, blocking collectives: 122 us -> none  [on_device(): row_max = lax.pmax(jnp.max(scores, axis=1), 'comp')]
    psum x1 -> x0, waiting for transfers between devices: 82.2 us -> none  [on_device(): summed_moments, summed_counts = lax.psum((moments, counts), 'dp')]
    ppermute x0 -> x13, starting transfers between devices: none -> 58.7 us  [the longest x5 27.3 us: row_logsumexp_stats(): lax.ppermute(jnp.stack([row_max, row_sum]), axis, xor_pairs(size, bit))]
    ppermute x0 -> x13, waiting for transfers between devices: none -> 49.7 us  [the longest x4 24.9 us: halving_psum(): current = keep + lax.ppermute(send, axis, xor_pairs(size, bit))]
  transfers between devices with their start and end apart: 1 -> 13, of which waited for: 1 -> 12; matrix products, arithmetic and copies ran while one was open for 1% -> 1% of each run, Pallas kernels for 0% -> 0%
where the time goes in v2:
time: 161 us; the launch traced here: 160 us
  starting transfers between devices  58.7 us (36%)
  waiting for transfers between devices  49.7 us (31%)
  matrix products  25.3 us (16%)
  other arithmetic  24 us (15%)
    ppermute x5, starting transfers between devices, row_logsumexp_stats(): lax.ppermute(jnp.stack([row_max, row_sum]), axis, xor_pairs(size, bit))  27.3 us
    ppermute x4, waiting for transfers between devices, halving_psum(): current = keep + lax.ppermute(send, axis, xor_pairs(size, bit))  24.9 us
    dot_general x8, matrix products, score_block(): lax.dot_general(features, loading, (((1,), (1,)), ((), ())), precision=la...  22.9 us
    ppermute x4, waiting for transfers between devices, halving_psum(): other = lax.ppermute(current, axis, xor_pairs(size, bit))  19.6 us
    ppermute x4, starting transfers between devices, halving_psum(): current = keep + lax.ppermute(send, axis, xor_pairs(size, bit))  18.8 us
    ppermute x4, starting transfers between devices, halving_psum(): other = lax.ppermute(current, axis, xor_pairs(size, bit))  12.5 us
    ppermute x5, waiting for transfers between devices, row_logsumexp_stats(): lax.ppermute(jnp.stack([row_max, row_sum]), axis, xor_pairs(size, bit))  5.16 us
    reduce_sum x1, other arithmetic, on_device(): local_sum = jnp.sum(jnp.exp(scores - local_max[:, None]), axis=1)  4.42 us
  transfers between devices with their start and end apart: 13, of which 12 were waited for; matrix products, arithmetic and copies ran while one was open for 1% of the time, Pallas kernels for 0%

profile of v2, /device:TPU:1, one launch (start us, length us, event | category | flops | bytes accessed | tf_op | source)
XLA Modules:
  0.0 160.2 jit_solution(5145727769847560810)
XLA Ops:
  0.7 1.6 %add_reduce_fusion = (f32[512]{0:T(512)S(1)}, f32[512,256]{1,0:T(8,128)S(1)}, f32[512,256]{1,0:T(8,128)S(1)}) fusion(f32[512,256]{1,0:T(8,128)} %param.8, f32[512,256]{1,0:T(8,128)} %param.7), kind=kLoop, calls=%fused_computation.28 | loop fusion | flops 916992 | bytes 2099200 | tf_op jit(solution)/shard_map/reduce_sum | solution.py:73
  2.3 0.1 pad_maximum_fusion
  2.6 23.7 %while.10 = (s32[]{:T(128)}, f32[8,512,512]{2,1,0:T(8,128)}, bf16[8,512,256]{2,1,0:T(8,128)(2,1)S(1)}, f32[512,512]{1,0:T(8,128)S(1)}, f32[512]{0:T(512)S(1)}, /*index=5*/s32[]{:T(128)}) while((s32[]{:T(128)}, f32[8,512,512]{2,1,0:T(8,128)}, bf16[8,512,256]{2,1,0:T(8,128)(2,1)S(1)}, f32[512,512]{1,0:T(8,128)S(1)}, f32[512]{0:T(512)S(1)}, ...), condition=%wide.region_2.3_spmd, body=%wide.region_1.2_spmd.sunk | while | flops 1611530240 | bytes 4721229 | solution.py:93
  2.6 2.9 %fusion.49 = f32[8,512,512]{2,1,0:T(8,128)} fusion(f32[8,512,512]{2,1,0:T(8,128)} %get-tuple-element.120, s32[]{:T(128)} %get-tuple-element.119, f32[512,512]{1,0:T(8,128)S(1)} %get-tuple-element.128, f32[512,256]{1,0:T(8,128)S(1)} %bitcast_convert_fusion.2, f32[512,256]{1,0:T(8,128)S(1)} %fusion.48, f32[512]{0:T(512)S(1)} %get-tuple-element.129), kind=kOutput, calls=%fused_computation.2.clone.1 | convolution fusion | flops 1611137024 | bytes 3148288 | tf_op jit(solution)/shard_map/while/body/eval_jaxpr/dot_general | solution.py:83
  5.6 2.9 %fusion.49 = f32[8,512,512]{2,1,0:T(8,128)} fusion(f32[8,512,512]{2,1,0:T(8,128)} %get-tuple-element.120, s32[]{:T(128)} %get-tuple-element.119, f32[512,512]{1,0:T(8,128)S(1)} %get-tuple-element.128, f32[512,256]{1,0:T(8,128)S(1)} %bitcast_convert_fusion.2, f32[512,256]{1,0:T(8,128)S(1)} %fusion.48, f32[512]{0:T(512)S(1)} %get-tuple-element.129), kind=kOutput, calls=%fused_computation.2.clone.1 | convolution fusion | flops 1611137024 | bytes 3148288 | tf_op jit(solution)/shard_map/while/body/eval_jaxpr/dot_general | solution.py:83
  8.6 2.9 %fusion.49 = f32[8,512,512]{2,1,0:T(8,128)} fusion(f32[8,512,512]{2,1,0:T(8,128)} %get-tuple-element.120, s32[]{:T(128)} %get-tuple-element.119, f32[512,512]{1,0:T(8,128)S(1)} %get-tuple-element.128, f32[512,256]{1,0:T(8,128)S(1)} %bitcast_convert_fusion.2, f32[512,256]{1,0:T(8,128)S(1)} %fusion.48, f32[512]{0:T(512)S(1)} %get-tuple-element.129), kind=kOutput, calls=%fused_computation.2.clone.1 | convolution fusion | flops 1611137024 | bytes 3148288 | tf_op jit(solution)/shard_map/while/body/eval_jaxpr/dot_general | solution.py:83
  11.6 2.9 %fusion.49 = f32[8,512,512]{2,1,0:T(8,128)} fusion(f32[8,512,512]{2,1,0:T(8,128)} %get-tuple-element.120, s32[]{:T(128)} %get-tuple-element.119, f32[512,512]{1,0:T(8,128)S(1)} %get-tuple-element.128, f32[512,256]{1,0:T(8,128)S(1)} %bitcast_convert_fusion.2, f32[512,256]{1,0:T(8,128)S(1)} %fusion.48, f32[512]{0:T(512)S(1)} %get-tuple-element.129), kind=kOutput, calls=%fused_computation.2.clone.1 | convolution fusion | flops 1611137024 | bytes 3148288 | tf_op jit(solution)/shard_map/while/body/eval_jaxpr/dot_general | solution.py:83
  14.5 2.8 %fusion.49 = f32[8,512,512]{2,1,0:T(8,128)} fusion(f32[8,512,512]{2,1,0:T(8,128)} %get-tuple-element.120, s32[]{:T(128)} %get-tuple-element.119, f32[512,512]{1,0:T(8,128)S(1)} %get-tuple-element.128, f32[512,256]{1,0:T(8,128)S(1)} %bitcast_convert_fusion.2, f32[512,256]{1,0:T(8,128)S(1)} %fusion.48, f32[512]{0:T(512)S(1)} %get-tuple-element.129), kind=kOutput, calls=%fused_computation.2.clone.1 | convolution fusion | flops 1611137024 | bytes 3148288 | tf_op jit(solution)/shard_map/while/body/eval_jaxpr/dot_general | solution.py:83
  17.4 2.9 %fusion.49 = f32[8,512,512]{2,1,0:T(8,128)} fusion(f32[8,512,512]{2,1,0:T(8,128)} %get-tuple-element.120, s32[]{:T(128)} %get-tuple-element.119, f32[512,512]{1,0:T(8,128)S(1)} %get-tuple-element.128, f32[512,256]{1,0:T(8,128)S(1)} %bitcast_convert_fusion.2, f32[512,256]{1,0:T(8,128)S(1)} %fusion.48, f32[512]{0:T(512)S(1)} %get-tuple-element.129), kind=kOutput, calls=%fused_computation.2.clone.1 | convolution fusion | flops 1611137024 | bytes 3148288 | tf_op jit(solution)/shard_map/while/body/eval_jaxpr/dot_general | solution.py:83
  20.4 2.9 %fusion.49 = f32[8,512,512]{2,1,0:T(8,128)} fusion(f32[8,512,512]{2,1,0:T(8,128)} %get-tuple-element.120, s32[]{:T(128)} %get-tuple-element.119, f32[512,512]{1,0:T(8,128)S(1)} %get-tuple-element.128, f32[512,256]{1,0:T(8,128)S(1)} %bitcast_convert_fusion.2, f32[512,256]{1,0:T(8,128)S(1)} %fusion.48, f32[512]{0:T(512)S(1)} %get-tuple-element.129), kind=kOutput, calls=%fused_computation.2.clone.1 | convolution fusion | flops 1611137024 | bytes 3148288 | tf_op jit(solution)/shard_map/while/body/eval_jaxpr/dot_general | solution.py:83
  23.4 2.8 %fusion.49 = f32[8,512,512]{2,1,0:T(8,128)} fusion(f32[8,512,512]{2,1,0:T(8,128)} %get-tuple-element.120, s32[]{:T(128)} %get-tuple-element.119, f32[512,512]{1,0:T(8,128)S(1)} %get-tuple-element.128, f32[512,256]{1,0:T(8,128)S(1)} %bitcast_convert_fusion.2, f32[512,256]{1,0:T(8,128)S(1)} %fusion.48, f32[512]{0:T(512)S(1)} %get-tuple-element.129), kind=kOutput, calls=%fused_computation.2.clone.1 | convolution fusion | flops 1611137024 | bytes 3148288 | tf_op jit(solution)/shard_map/while/body/eval_jaxpr/dot_general | solution.py:83
  26.3 4.0 %reduce_max.11 = f32[8,512]{1,0:T(8,128)S(1)} reduce(f32[8,512,512]{2,1,0:T(8,128)} %get-tuple-element.30, f32[]{:T(128)} %constant.113.clone.1), dimensions={2}, to_apply=%region_3.4 | reduce | flops 2093056 | bytes 8404996 | tf_op jit(solution)/shard_map/reduce_max | solution.py:94
  30.3 4.4 %exponential_reduce_fusion.1 = f32[8,512]{1,0:T(8,128)S(1)} fusion(f32[8,512,512]{2,1,0:T(8,128)} %get-tuple-element.30, f32[8,512]{1,0:T(8,128)S(1)} %reduce_max.11), kind=kLoop, calls=%fused_computation.13 | loop fusion | flops 4190208 | bytes 8421376 | tf_op jit(solution)/shard_map/reduce_sum | solution.py:95
  34.8 3.9 %collective-permute-start = (f32[2,4096]{1,0:T(2,128)S(1)}, f32[2,4096]{1,0:T(2,128)S(1)}, u32[]{:S(2)}, u32[]{:S(2)}) collective-permute-start(f32[2,4096]{1,0:T(2,128)S(1)} %pad_maximum_fusion.1), channel_id=1, source_target_pairs={{0,1},{1,0},{2,3},{3,2},{4,5},{5,4},{6,7},{7,6},{8,9},{9,8},{10,11... | collective-permute-start | bytes 98312 | tf_op jit(solution)/shard_map/ppermute | solution.py:30
  38.7 1.3 collective-permute-done
  40.0 0.1 slice_reduce_fusion.9
  40.2 4.9 %collective-permute-start.1 = (f32[2,4096]{1,0:T(2,128)S(1)}, f32[2,4096]{1,0:T(2,128)S(1)}, u32[]{:S(2)}, u32[]{:S(2)}) collective-permute-start(f32[2,4096]{1,0:T(2,128)S(1)} %pad_maximum_fusion.2), channel_id=1, source_target_pairs={{0,2},{1,3},{2,0},{3,1},{4,6},{5,7},{6,4},{7,5},{8,10},{9,11},{10,... | collective-permute-start | bytes 98312 | tf_op jit(solution)/shard_map/ppermute | solution.py:30
  45.1 1.3 collective-permute-done.1
  46.4 0.1 slice_reduce_fusion.8
  46.6 4.2 %collective-permute-start.2 = (f32[2,4096]{1,0:T(2,128)S(1)}, f32[2,4096]{1,0:T(2,128)S(1)}, u32[]{:S(2)}, u32[]{:S(2)}) collective-permute-start(f32[2,4096]{1,0:T(2,128)S(1)} %pad_maximum_fusion.3), channel_id=1, source_target_pairs={{0,4},{1,5},{2,6},{3,7},{4,0},{5,1},{6,2},{7,3},{8,12},{9,13},{10,... | collective-permute-start | bytes 98312 | tf_op jit(solution)/shard_map/ppermute | solution.py:30
  50.8 1.3 collective-permute-done.2
  52.2 5.8 %collective-permute-start.3 = (f32[2,4096]{1,0:T(2,128)S(1)}, f32[2,4096]{1,0:T(2,128)S(1)}, u32[]{:S(2)}, u32[]{:S(2)}) collective-permute-start(f32[2,4096]{1,0:T(2,128)S(1)} %pad_maximum_fusion.4), channel_id=1, source_target_pairs={{0,8},{1,9},{2,10},{3,11},{4,12},{5,13},{6,14},{7,15},{8,0},{9,1},... | collective-permute-start | bytes 98312 | tf_op jit(solution)/shard_map/ppermute | solution.py:30
  58.1 1.3 collective-permute-done.3
  59.5 8.4 %collective-permute-start.4 = (f32[2,4096]{1,0:T(2,128)S(1)}, f32[2,4096]{1,0:T(2,128)S(1)}, u32[]{:S(2)}, u32[]{:S(2)}) collective-permute-start(f32[2,4096]{1,0:T(2,128)S(1)} %pad_maximum_fusion.5), channel_id=1, source_target_pairs={{0,16},{1,17},{2,18},{3,19},{4,20},{5,21},{6,22},{7,23},{8,24},{9,... | collective-permute-start | bytes 98312 | tf_op jit(solution)/shard_map/ppermute | solution.py:30
  68.0 1.8 %multiply_convert_fusion = bf16[4096,256]{1,0:T(8,128)(2,1)} fusion(bf16[4096,256]{1,0:T(8,128)(2,1)S(1)} %bitcast.52), kind=kLoop, calls=%fused_computation.18 | loop fusion | flops 3145728 | bytes 4194304 | tf_op jit(solution)/shard_map/convert_element_type | solution.py:102
  70.1 4.2 %fusion.8 = bf16[4096,512]{1,0:T(8,128)(2,1)S(1)} fusion(f32[8,512,512]{2,1,0:T(8,128)} %get-tuple-element.30, f32[4096]{0:T(1024)S(1)} %log_add_fusion.1), kind=kLoop, calls=%fused_computation.11 | loop fusion | flops 4194304 | bytes 12599296 | tf_op jit(solution)/shard_map/convert_element_type | solution.py:100
  74.3 2.3 %fusion.9 = f32[512,512]{1,0:T(8,128)S(1)} fusion(bf16[4096,512]{1,0:T(8,128)(2,1)S(1)} %fusion.8, bf16[4096,256]{1,0:T(8,128)(2,1)S(1)} %copy-done.1, bf16[4096,256]{1,0:T(8,128)(2,1)S(1)} %bitcast.53), kind=kOutput, calls=%fused_computation.14 | convolution fusion | flops 2155872256 | bytes 9437184 | tf_op jit(solution)/shard_map/dot_general | solution.py:103
  76.9 4.1 %exponential_reduce_fusion = f32[512]{0:T(512)S(1)} fusion(f32[8,512,512]{2,1,0:T(8,128)} %get-tuple-element.30, f32[8,512]{1,0:T(8,128)S(1)} %log_add_fusion), kind=kLoop, calls=%fused_computation.12 | loop fusion | flops 4193792 | bytes 8407040 | tf_op jit(solution)/shard_map/reduce_sum | solution.py:99
  81.1 0.5 concatenate.38
  81.6 10.0 %collective-permute-start.5 = (f32[1088,128]{1,0:T(8,128)S(1)}, f32[1088,128]{1,0:T(8,128)S(1)}, u32[]{:S(2)}, u32[]{:S(2)}) collective-permute-start(f32[1088,128]{1,0:T(8,128)S(1)} %slice_select_fusion), channel_id=1, source_target_pairs={{0,32},{32,0},{64,96},{96,64},{128,160},{160,128},{192,224},{224,1... | collective-permute-start | bytes 1671176 | tf_op jit(solution)/shard_map/ppermute | solution.py:51
  91.6 1.5 collective-permute-done.5
  93.3 1.9 %collective-permute-start.6 = (f32[544,128]{1,0:T(8,128)S(1)}, f32[544,128]{1,0:T(8,128)S(1)}, u32[]{:S(2)}, u32[]{:S(2)}) collective-permute-start(f32[544,128]{1,0:T(8,128)S(1)} %slice_select_fusion.1), channel_id=1, source_target_pairs={{0,64},{32,96},{64,0},{96,32},{128,192},{160,224},{192,128},{224,1... | collective-permute-start | bytes 835592 | tf_op jit(solution)/shard_map/ppermute | solution.py:51
  95.3 7.8 %collective-permute-done.6 = f32[544,128]{1,0:T(8,128)S(1)} collective-permute-done((f32[544,128]{1,0:T(8,128)S(1)}, f32[544,128]{1,0:T(8,128)S(1)}, u32[]{:S(2)}, u32[]{:S(2)}) %collective-permute-start.6) | collective-permute-done | bytes 278560 | tf_op jit(solution)/shard_map/ppermute | solution.py:51
  103.1 1.9 %collective-permute-start.7 = (f32[272,128]{1,0:T(8,128)S(1)}, f32[272,128]{1,0:T(8,128)S(1)}, u32[]{:S(2)}, u32[]{:S(2)}) collective-permute-start(f32[272,128]{1,0:T(8,128)S(1)} %slice_select_fusion.2), channel_id=1, source_target_pairs={{0,128},{32,160},{64,192},{96,224},{128,0},{160,32},{192,64},{224,... | collective-permute-start | bytes 417800 | tf_op jit(solution)/shard_map/ppermute | solution.py:51
  105.1 9.4 %collective-permute-done.7 = f32[272,128]{1,0:T(8,128)S(1)} collective-permute-done((f32[272,128]{1,0:T(8,128)S(1)}, f32[272,128]{1,0:T(8,128)S(1)}, u32[]{:S(2)}, u32[]{:S(2)}) %collective-permute-start.7) | collective-permute-done | bytes 139296 | tf_op jit(solution)/shard_map/ppermute | solution.py:51
  114.5 5.0 %collective-permute-start.8 = (f32[136,128]{1,0:T(8,128)S(1)}, f32[136,128]{1,0:T(8,128)S(1)}, u32[]{:S(2)}, u32[]{:S(2)}) collective-permute-start(f32[136,128]{1,0:T(8,128)S(1)} %slice_select_fusion.3), channel_id=1, source_target_pairs={{0,256},{32,288},{64,320},{96,352},{128,384},{160,416},{192,448},{... | collective-permute-start | bytes 208904 | tf_op jit(solution)/shard_map/ppermute | solution.py:51
  119.6 6.2 %collective-permute-done.8 = f32[136,128]{1,0:T(8,128)S(1)} collective-permute-done((f32[136,128]{1,0:T(8,128)S(1)}, f32[136,128]{1,0:T(8,128)S(1)}, u32[]{:S(2)}, u32[]{:S(2)}) %collective-permute-start.8) | collective-permute-done | bytes 69664 | tf_op jit(solution)/shard_map/ppermute | solution.py:51
  125.8 4.3 %collective-permute-start.9 = (f32[136,128]{1,0:T(8,128)S(1)}, f32[136,128]{1,0:T(8,128)S(1)}, u32[]{:S(2)}, u32[]{:S(2)}) collective-permute-start(f32[136,128]{1,0:T(8,128)S(1)} %select_add_fusion.3), channel_id=1, source_target_pairs={{0,256},{32,288},{64,320},{96,352},{128,384},{160,416},{192,448},{... | collective-permute-start | bytes 208904 | tf_op jit(solution)/shard_map/ppermute | solution.py:56
  130.2 6.1 %collective-permute-done.9 = f32[136,128]{1,0:T(8,128)S(1)} collective-permute-done((f32[136,128]{1,0:T(8,128)S(1)}, f32[136,128]{1,0:T(8,128)S(1)}, u32[]{:S(2)}, u32[]{:S(2)}) %collective-permute-start.9) | collective-permute-done | bytes 69664 | tf_op jit(solution)/shard_map/ppermute | solution.py:56
  136.3 1.9 %collective-permute-start.10 = (f32[272,128]{1,0:T(8,128)S(1)}, f32[272,128]{1,0:T(8,128)S(1)}, u32[]{:S(2)}, u32[]{:S(2)}) collective-permute-start(f32[272,128]{1,0:T(8,128)S(1)} %maximum_select_fusion.3), channel_id=1, source_target_pairs={{0,128},{32,160},{64,192},{96,224},{128,0},{160,32},{192,64},{224,... | collective-permute-start | bytes 417800 | tf_op jit(solution)/shard_map/ppermute | solution.py:56
  138.2 5.4 %collective-permute-done.10 = f32[272,128]{1,0:T(8,128)S(1)} collective-permute-done((f32[272,128]{1,0:T(8,128)S(1)}, f32[272,128]{1,0:T(8,128)S(1)}, u32[]{:S(2)}, u32[]{:S(2)}) %collective-permute-start.10) | collective-permute-done | bytes 139296 | tf_op jit(solution)/shard_map/ppermute | solution.py:56
  143.6 1.9 %collective-permute-start.11 = (f32[544,128]{1,0:T(8,128)S(1)}, f32[544,128]{1,0:T(8,128)S(1)}, u32[]{:S(2)}, u32[]{:S(2)}) collective-permute-start(f32[544,128]{1,0:T(8,128)S(1)} %maximum_select_fusion.2), channel_id=1, source_target_pairs={{0,64},{32,96},{64,0},{96,32},{128,192},{160,224},{192,128},{224,1... | collective-permute-start | bytes 835592 | tf_op jit(solution)/shard_map/ppermute | solution.py:56
  145.6 6.6 %collective-permute-done.11 = f32[544,128]{1,0:T(8,128)S(1)} collective-permute-done((f32[544,128]{1,0:T(8,128)S(1)}, f32[544,128]{1,0:T(8,128)S(1)}, u32[]{:S(2)}, u32[]{:S(2)}) %collective-permute-start.11) | collective-permute-done | bytes 278560 | tf_op jit(solution)/shard_map/ppermute | solution.py:56
  152.2 4.4 %collective-permute-start.12 = (f32[1088,128]{1,0:T(8,128)S(1)}, f32[1088,128]{1,0:T(8,128)S(1)}, u32[]{:S(2)}, u32[]{:S(2)}) collective-permute-start(f32[1088,128]{1,0:T(8,128)S(1)} %maximum_select_fusion.1), channel_id=1, source_target_pairs={{0,32},{32,0},{64,96},{96,64},{128,160},{160,128},{192,224},{224,1... | collective-permute-start | bytes 1671176 | tf_op jit(solution)/shard_map/ppermute | solution.py:56
  156.6 1.6 collective-permute-done.12
  158.3 0.6 log_add_fusion.2
  158.9 0.2 reshape.202
  159.1 1.2 fusion.14
  (71 shorter events, 2.2 us)
Async XLA Ops:
  0.6 1.8 %copy-start.4 = (f32[512]{0:T(512)S(1)}, f32[512]{0:T(512)}, u32[]{:S(2)}) copy-start(f32[512]{0:T(512)} %param.9) | copy-start | bytes 6148
  0.6 1.9 %copy-start = (bf16[4096,256]{1,0:T(8,128)(2,1)S(1)}, bf16[4096,256]{1,0:T(8,128)(2,1)}, u32[]{:S(2)}) copy-start(bf16[4096,256]{1,0:T(8,128)(2,1)} %param.6) | copy-start | bytes 6291460
  34.8 5.2 %collective-permute-start = (f32[2,4096]{1,0:T(2,128)S(1)}, f32[2,4096]{1,0:T(2,128)S(1)}, u32[]{:S(2)}, u32[]{:S(2)}) collective-permute-start(f32[2,4096]{1,0:T(2,128)S(1)} %pad_maximum_fusion.1), channel_id=1, source_target_pairs={{0,1},{1,0},{2,3},{3,2},{4,5},{5,4},{6,7},{7,6},{8,9},{9,8},{10,11... | collective-permute-start | bytes 98312 | tf_op jit(solution)/shard_map/ppermute | solution.py:30
  40.2 6.2 %collective-permute-start.1 = (f32[2,4096]{1,0:T(2,128)S(1)}, f32[2,4096]{1,0:T(2,128)S(1)}, u32[]{:S(2)}, u32[]{:S(2)}) collective-permute-start(f32[2,4096]{1,0:T(2,128)S(1)} %pad_maximum_fusion.2), channel_id=1, source_target_pairs={{0,2},{1,3},{2,0},{3,1},{4,6},{5,7},{6,4},{7,5},{8,10},{9,11},{10,... | collective-permute-start | bytes 98312 | tf_op jit(solution)/shard_map/ppermute | solution.py:30
  46.6 5.5 %collective-permute-start.2 = (f32[2,4096]{1,0:T(2,128)S(1)}, f32[2,4096]{1,0:T(2,128)S(1)}, u32[]{:S(2)}, u32[]{:S(2)}) collective-permute-start(f32[2,4096]{1,0:T(2,128)S(1)} %pad_maximum_fusion.3), channel_id=1, source_target_pairs={{0,4},{1,5},{2,6},{3,7},{4,0},{5,1},{6,2},{7,3},{8,12},{9,13},{10,... | collective-permute-start | bytes 98312 | tf_op jit(solution)/shard_map/ppermute | solution.py:30
  52.2 7.1 %collective-permute-start.3 = (f32[2,4096]{1,0:T(2,128)S(1)}, f32[2,4096]{1,0:T(2,128)S(1)}, u32[]{:S(2)}, u32[]{:S(2)}) collective-permute-start(f32[2,4096]{1,0:T(2,128)S(1)} %pad_maximum_fusion.4), channel_id=1, source_target_pairs={{0,8},{1,9},{2,10},{3,11},{4,12},{5,13},{6,14},{7,15},{8,0},{9,1},... | collective-permute-start | bytes 98312 | tf_op jit(solution)/shard_map/ppermute | solution.py:30
  59.5 10.4 %collective-permute-start.4 = (f32[2,4096]{1,0:T(2,128)S(1)}, f32[2,4096]{1,0:T(2,128)S(1)}, u32[]{:S(2)}, u32[]{:S(2)}) collective-permute-start(f32[2,4096]{1,0:T(2,128)S(1)} %pad_maximum_fusion.5), channel_id=1, source_target_pairs={{0,16},{1,17},{2,18},{3,19},{4,20},{5,21},{6,22},{7,23},{8,24},{9,... | collective-permute-start | bytes 98312 | tf_op jit(solution)/shard_map/ppermute | solution.py:30
  70.1 4.3 %copy-start.1 = (bf16[4096,256]{1,0:T(8,128)(2,1)S(1)}, bf16[4096,256]{1,0:T(8,128)(2,1)}, u32[]{:S(2)}) copy-start(bf16[4096,256]{1,0:T(8,128)(2,1)} %multiply_convert_fusion) | copy-start | bytes 6291460
  81.6 11.5 %collective-permute-start.5 = (f32[1088,128]{1,0:T(8,128)S(1)}, f32[1088,128]{1,0:T(8,128)S(1)}, u32[]{:S(2)}, u32[]{:S(2)}) collective-permute-start(f32[1088,128]{1,0:T(8,128)S(1)} %slice_select_fusion), channel_id=1, source_target_pairs={{0,32},{32,0},{64,96},{96,64},{128,160},{160,128},{192,224},{224,1... | collective-permute-start | bytes 1671176 | tf_op jit(solution)/shard_map/ppermute | solution.py:51
  93.3 9.7 %collective-permute-start.6 = (f32[544,128]{1,0:T(8,128)S(1)}, f32[544,128]{1,0:T(8,128)S(1)}, u32[]{:S(2)}, u32[]{:S(2)}) collective-permute-start(f32[544,128]{1,0:T(8,128)S(1)} %slice_select_fusion.1), channel_id=1, source_target_pairs={{0,64},{32,96},{64,0},{96,32},{128,192},{160,224},{192,128},{224,1... | collective-permute-start | bytes 835592 | tf_op jit(solution)/shard_map/ppermute | solution.py:51
  103.1 11.4 %collective-permute-start.7 = (f32[272,128]{1,0:T(8,128)S(1)}, f32[272,128]{1,0:T(8,128)S(1)}, u32[]{:S(2)}, u32[]{:S(2)}) collective-permute-start(f32[272,128]{1,0:T(8,128)S(1)} %slice_select_fusion.2), channel_id=1, source_target_pairs={{0,128},{32,160},{64,192},{96,224},{128,0},{160,32},{192,64},{224,... | collective-permute-start | bytes 417800 | tf_op jit(solution)/shard_map/ppermute | solution.py:51
  114.5 11.3 %collective-permute-start.8 = (f32[136,128]{1,0:T(8,128)S(1)}, f32[136,128]{1,0:T(8,128)S(1)}, u32[]{:S(2)}, u32[]{:S(2)}) collective-permute-start(f32[136,128]{1,0:T(8,128)S(1)} %slice_select_fusion.3), channel_id=1, source_target_pairs={{0,256},{32,288},{64,320},{96,352},{128,384},{160,416},{192,448},{... | collective-permute-start | bytes 208904 | tf_op jit(solution)/shard_map/ppermute | solution.py:51
  125.8 33.3 %copy-start.2 = (f32[512,256]{1,0:T(8,128)S(1)}, f32[512,256]{1,0:T(8,128)}, u32[]{:S(2)}) copy-start(f32[512,256]{1,0:T(8,128)} %param.8) | copy-start | bytes 1572868
  125.8 33.3 %copy-start.3 = (f32[512,256]{1,0:T(8,128)S(1)}, f32[512,256]{1,0:T(8,128)}, u32[]{:S(2)}) copy-start(f32[512,256]{1,0:T(8,128)} %param.7) | copy-start | bytes 1572868
  125.8 10.4 %collective-permute-start.9 = (f32[136,128]{1,0:T(8,128)S(1)}, f32[136,128]{1,0:T(8,128)S(1)}, u32[]{:S(2)}, u32[]{:S(2)}) collective-permute-start(f32[136,128]{1,0:T(8,128)S(1)} %select_add_fusion.3), channel_id=1, source_target_pairs={{0,256},{32,288},{64,320},{96,352},{128,384},{160,416},{192,448},{... | collective-permute-start | bytes 208904 | tf_op jit(solution)/shard_map/ppermute | solution.py:56
  136.3 7.3 %collective-permute-start.10 = (f32[272,128]{1,0:T(8,128)S(1)}, f32[272,128]{1,0:T(8,128)S(1)}, u32[]{:S(2)}, u32[]{:S(2)}) collective-permute-start(f32[272,128]{1,0:T(8,128)S(1)} %maximum_select_fusion.3), channel_id=1, source_target_pairs={{0,128},{32,160},{64,192},{96,224},{128,0},{160,32},{192,64},{224,... | collective-permute-start | bytes 417800 | tf_op jit(solution)/shard_map/ppermute | solution.py:56
  143.6 8.5 %collective-permute-start.11 = (f32[544,128]{1,0:T(8,128)S(1)}, f32[544,128]{1,0:T(8,128)S(1)}, u32[]{:S(2)}, u32[]{:S(2)}) collective-permute-start(f32[544,128]{1,0:T(8,128)S(1)} %maximum_select_fusion.2), channel_id=1, source_target_pairs={{0,64},{32,96},{64,0},{96,32},{128,192},{160,224},{192,128},{224,1... | collective-permute-start | bytes 835592 | tf_op jit(solution)/shard_map/ppermute | solution.py:56
  152.2 5.9 %collective-permute-start.12 = (f32[1088,128]{1,0:T(8,128)S(1)}, f32[1088,128]{1,0:T(8,128)S(1)}, u32[]{:S(2)}, u32[]{:S(2)}) collective-permute-start(f32[1088,128]{1,0:T(8,128)S(1)} %maximum_select_fusion.1), channel_id=1, source_target_pairs={{0,32},{32,0},{64,96},{96,64},{128,160},{160,128},{192,224},{224,1... | collective-permute-start | bytes 1671176 | tf_op jit(solution)/shard_map/ppermute | solution.py:56
